TPU v7x, 256 devices: a whole 4x4x8 slice. The times are simulated.
256 devices in a mesh: dp: 16 (over x, y), expert: 16 (over z, core).
Axes of the slice: x: 4, y: 4, z: 8, core: 2. Of those that a mesh axis runs over, the one named last changes fastest.
Arguments:
- hidden: bfloat16 [32768, 8, 768], P(('dp', 'expert')), may hold values from -6 to 6
- upstream: bfloat16 [32768, 4096], P(('dp', 'expert')), may hold values from -0.125 to 0.125
- probs: bfloat16 [32768, 8], P(('dp', 'expert')), may hold values from 0.019897461 to 0.5
- expert_ids: int32 [32768, 8], P(('dp', 'expert')), may hold values from 0 to 15, all different within a row; in each aligned block of 128 rows (0 to 127, 128 to 255, ...) at most 72 rows name the same one
- w_down: bfloat16 [16, 4096, 768], P('expert', 'dp'), may hold values from -0.21875 to 0.21875
Outputs:
- grad_down: float32 [16, 4096, 768], P('expert', 'dp')
- gate_grad: float32 [32768, 8], P(('dp', 'expert'))
Inputs may be any that keep to these rules, and one draw needn't show every extreme that they name: `expert_ids`: each row names 8 different experts; among the rows of one device no expert is named by more than 72 rows, a bound that some block reaches.
All inputs are finite; a program needn't handle non-finite values.
Results may differ from a plain program's by a relative error of at most 0.013.
Values may be sent and summed in bfloat16 or wider, within the bound.
No kernel may reach another device: no remote copies, remote signals or barrier semaphores. Data moves between devices by JAX's collectives and lax.ppermute only.
A program may use at most 128 MiB of HBM per device.

v0:
```python
import jax
import jax.numpy as jnp
from jax import lax
from jax.sharding import Mesh, PartitionSpec as P


def body(hidden, upstream, probs, expert_ids, w_down):
    tok_rows, top_k = expert_ids.shape
    hid_width = hidden.shape[2]
    model_width = upstream.shape[1]
    n_z = lax.axis_size("z")
    n_core = lax.axis_size("core")
    n_dp = lax.axis_size("x") * lax.axis_size("y")
    groups = n_z * n_core
    slots_per = max(tok_rows * 9 // 16, tok_rows * top_k // groups)
    total_rows = groups * slots_per
    ez = ("z", "core")
    chosen = (expert_ids[:, :, None] == jnp.arange(groups, dtype=jnp.int32)[None, None, :]).astype(
        jnp.int32
    )
    member = jnp.sum(chosen, axis=1)
    slot_place = jnp.cumsum(member, axis=0) - 1
    which_k = jnp.sum(chosen * jnp.arange(top_k, dtype=jnp.int32)[None, :, None], axis=1)
    target = (
        (member == 1)[:, :, None]
        & (slot_place[:, :, None] == jnp.arange(slots_per, dtype=jnp.int32)[None, None, :])
    ).astype(jnp.int32)
    filled = jnp.sum(target, axis=0) == 1
    source_tok = jnp.sum(target * jnp.arange(tok_rows, dtype=jnp.int32)[:, None, None], axis=0)
    source_k = jnp.sum(target * which_k[:, :, None], axis=0)
    flat_index = (source_tok * top_k + source_k).reshape(-1)
    picked_h = hidden.reshape(tok_rows * top_k, hid_width)[flat_index].reshape(
        groups, slots_per, hid_width
    )
    send_h = jnp.where(filled[:, :, None], picked_h, jnp.zeros_like(picked_h))
    routed = member == 1
    p_tok = jnp.sum(
        jnp.where(chosen == 1, probs.astype(jnp.float32)[:, :, None], jnp.float32(0.0)), axis=1
    )
    inv = jnp.where(routed, slot_place, -1).astype(jnp.float32)
    send_meta = jnp.stack([p_tok.T, inv.T], axis=1)
    dy_z = lax.all_gather(upstream, "z", axis=0, tiled=True)
    recv_h = lax.all_to_all(send_h, ez, split_axis=0, concat_axis=0, tiled=True)
    recv_meta = lax.all_to_all(send_meta, ez, split_axis=0, concat_axis=0, tiled=True)

    def ring_gather(x, axis):
        n = lax.axis_size(axis)
        got = [x] + [
            lax.ppermute(x, axis, perm=[(i, (i - d) % n) for i in range(n)]) for d in range(1, n)
        ]
        return jnp.roll(jnp.stack(got), lax.axis_index(axis), axis=0)

    w_full = ring_gather(ring_gather(w_down[0], "y"), "x")
    dy_z, w_full, recv_h, recv_meta = lax.optimization_barrier((dy_z, w_full, recv_h, recv_meta))
    w_full = w_full.reshape(-1, hid_width)
    dy_pair = lax.ppermute(dy_z, "core", perm=[(c, (c + 1) % n_core) for c in range(n_core)])
    my_core = lax.axis_index("core")
    other_core = (my_core + 1) % n_core

    def inputs(c):
        meta = lax.dynamic_index_in_dim(
            recv_meta.reshape(n_z, n_core, 2, tok_rows), c, axis=1, keepdims=False
        )
        p_c = meta[:, 0, :].reshape(-1)
        slot = meta[:, 1, :].astype(jnp.int32)
        h_src = lax.dynamic_index_in_dim(
            recv_h.reshape(n_z, n_core, slots_per, hid_width), c, axis=1, keepdims=False
        )
        pick = (slot[:, :, None] == jnp.arange(slots_per, dtype=jnp.int32)[None, None, :]).astype(
            h_src.dtype
        )
        h_c = lax.dot_general(
            pick, h_src, (((2,), (1,)), ((0,), (0,))), preferred_element_type=jnp.float32
        ).astype(h_src.dtype)
        return (p_c, h_c.reshape(n_z * tok_rows, hid_width))

    p_own, h_own = inputs(my_core)
    p_pair, h_pair = inputs(other_core)

    def part(dy_c, p_c, h_c):
        scaled = (p_c[:, None] * dy_c.astype(jnp.float32)).astype(jnp.bfloat16)
        return lax.dot_general(
            scaled, h_c, (((0,), (0,)), ((), ())), preferred_element_type=jnp.float32
        )

    def score(dy_c, h_c):
        g = lax.dot_general(
            dy_c, w_full, (((1,), (0,)), ((), ())), preferred_element_type=jnp.float32
        )
        return jnp.sum(g * h_c.astype(jnp.float32), axis=1).reshape(n_z, tok_rows)

    partial = (part(dy_z, p_own, h_own) + part(dy_pair, p_pair, h_pair)).astype(jnp.bfloat16)
    grad_block = lax.psum_scatter(partial, ("x", "y"), scatter_dimension=0, tiled=True).astype(
        jnp.float32
    )
    score_own = score(dy_z, h_own)
    score_pair = score(dy_pair, h_pair)
    first = jnp.where(my_core == 0, score_own, score_pair)
    second = jnp.where(my_core == 0, score_pair, score_own)
    by_source = jnp.stack([first, second], axis=1).reshape(groups, tok_rows)
    returned = lax.all_to_all(by_source, ez, split_axis=0, concat_axis=0, tiled=True)
    gate_grad = jnp.sum(
        jnp.where(
            expert_ids[:, :, None] == jnp.arange(groups, dtype=jnp.int32)[None, None, :],
            returned.T[:, None, :],
            jnp.float32(0.0),
        ),
        axis=2,
    )
    return (grad_block[None], gate_grad)


def solution(mesh):
    n_dp, n_expert = mesh.devices.shape
    side = 4 if n_dp % 4 == 0 else 1
    sub = Mesh(mesh.devices.reshape(n_dp // side, side, n_expert // 2, 2), ("x", "y", "z", "core"))
    tok = ("x", "y", "z", "core")
    in_specs = (
        P(tok, None, None),
        P(tok, None),
        P(tok, None),
        P(tok, None),
        P(("z", "core"), ("x", "y"), None),
    )
    out_specs = (P(("z", "core"), ("x", "y"), None), P(tok, None))
    return jax.shard_map(body, mesh=sub, in_specs=in_specs, out_specs=out_specs, check_vma=False)
```

profile of v0, /device:TPU:1, one launch (start us, length us, event | category | flops | bytes accessed | tf_op | source)
XLA Modules:
  0.0 267.1 jit_solution(8966174074436116329)
XLA Ops:
  7.9 3.6 %collective-permute-start = (bf16[256,768]{1,0:T(8,128)(2,1)}, bf16[256,768]{1,0:T(8,128)(2,1)S(1)}, u32[]{:S(2)}, u32[]{:S(2)}) collective-permute-start(bf16[256,768]{1,0:T(8,128)(2,1)} %bitcast.81), channel_id=1, source_target_pairs={{0,48},{16,0},{32,16},{48,32},{1,49},{17,1},{33,17},{49,33},{2,50}... | collective-permute-start | bytes 1179656 | tf_op jit(solution)/shard_map/ppermute | solution.py:49
  15.8 10.0 %all-to-all-start.1 = ((f32[16,2,128]{2,1,0:T(2,128)}), f32[16,2,128]{2,1,0:T(2,128)S(1)}, u32[]{:S(2)}, u32[]{:S(2)}) async-start(f32[16,2,128]{2,1,0:T(2,128)} %copy.33), calls=%async_computation.1 | async-start | bytes 32768 | tf_op jit(solution)/shard_map/all_to_all | solution.py:44
  28.1 4.8 %collective-permute-done.2 = bf16[256,768]{1,0:T(8,128)(2,1)S(1)} collective-permute-done((bf16[256,768]{1,0:T(8,128)(2,1)}, bf16[256,768]{1,0:T(8,128)(2,1)S(1)}, u32[]{:S(2)}, u32[]{:S(2)}) %collective-permute-start.2) | collective-permute-done | bytes 393248 | tf_op jit(solution)/shard_map/ppermute | solution.py:49
  33.0 1.9 bitcast_dynamic-update-slice_fusion.6
  34.9 2.5 collective-permute-start.3
  38.1 4.6 %gather_fusion = bf16[1152,768]{1,0:T(8,128)(2,1)S(1)} fusion(bf16[1024,768]{1,0:T(8,128)(2,1)S(1)} %bitcast.71, s32[2048]{0:T(1024)S(1)} %pad_clamp_fusion), kind=kCustom, calls=%fused_computation | custom fusion | bytes 3543552 | tf_op jit(solution)/shard_map/gather | solution.py:32
  43.3 1.4 broadcast_select_fusion
  44.7 9.7 %all-to-all-start = ((bf16[16,72,768]{2,1,0:T(8,128)(2,1)}), bf16[16,72,768]{2,1,0:T(8,128)(2,1)S(1)}, u32[]{:S(2)}, u32[]{:S(2)}) async-start(bf16[16,72,768]{2,1,0:T(8,128)(2,1)} %broadcast_select_fusion), calls=%async_computation | async-start | bytes 3538944 | tf_op jit(solution)/shard_map/all_to_all | solution.py:43
  54.5 50.2 %collective-permute-done.3 = bf16[4,256,768]{2,1,0:T(8,128)(2,1)} collective-permute-done((bf16[4,256,768]{2,1,0:T(8,128)(2,1)}, bf16[4,256,768]{2,1,0:T(8,128)(2,1)}, u32[]{:S(2)}, u32[]{:S(2)}) %collective-permute-start.3) | collective-permute-done | bytes 1572896 | tf_op jit(solution)/shard_map/ppermute | solution.py:49
  104.7 2.7 bitcast_dynamic-update-slice_fusion.4
  107.3 2.6 bitcast_dynamic-update-slice_fusion.2
  111.3 2.7 %bitcast_dynamic-update-slice_fusion.7 = bf16[8,4,256,768]{3,2,1,0:T(8,128)(2,1)} fusion(bf16[8,4,256,768]{3,2,1,0:T(8,128)(2,1)} %bitcast_dynamic-update-slice_fusion, bf16[4,256,768]{2,1,0:T(8,128)(2,1)} %get-tuple-element.18), kind=kLoop, calls=%fused_computation.20 | loop fusion | bytes 3145728
  113.9 2.7 %bitcast_dynamic-update-slice_fusion.5 = bf16[8,4,256,768]{3,2,1,0:T(8,128)(2,1)} fusion(bf16[8,4,256,768]{3,2,1,0:T(8,128)(2,1)} %bitcast_dynamic-update-slice_fusion.7, bf16[4,256,768]{2,1,0:T(8,128)(2,1)} %collective-permute-done.3), kind=kLoop, calls=%fused_computation.18 | loop fusion | bytes 3145728
  116.7 2.7 %bitcast_dynamic-update-slice_fusion.3 = bf16[8,4,256,768]{3,2,1,0:T(8,128)(2,1)} fusion(bf16[8,4,256,768]{3,2,1,0:T(8,128)(2,1)} %bitcast_dynamic-update-slice_fusion.5, bf16[4,256,768]{2,1,0:T(8,128)(2,1)} %collective-permute-done.4), kind=kLoop, calls=%fused_computation.16 | loop fusion | bytes 3145728
  120.6 6.1 %constant_dynamic-slice_fusion.2 = bf16[4,4,256,768]{3,2,1,0:T(8,128)(2,1)} fusion(bf16[8,4,256,768]{3,2,1,0:T(8,128)(2,1)} %bitcast_dynamic-update-slice_fusion.1, s32[]{:T(128)S(6)} %select_n.102), kind=kLoop, calls=%fused_computation.71 | loop fusion | bytes 12582916 | tf_op jit(solution)/shard_map/jit(_roll_dynamic)/dynamic_slice | solution.py:51
  126.7 19.4 %all-gather.2.cloned.1.call-done = bf16[1024,4096]{1,0:T(8,128)(2,1)} async-done(((bf16[128,4096]{1,0:T(8,128)(2,1)}), bf16[1024,4096]{1,0:T(8,128)(2,1)}) %all-gather.2.cloned.1.call-update) | async-done | bytes 8388624 | tf_op jit(solution)/shard_map/all_gather | solution.py:42
  148.1 10.8 %fusion = f32[4096,768]{1,0:T(8,128)S(1)} fusion(bf16[1024,768]{1,0:T(8,128)(2,1)S(1)} %bitcast.79, bf16[1024,4096]{1,0:T(8,128)(2,1)} %all-gather.2.cloned.1.call-done, f32[1024]{0:T(1024)S(1)} %get-tuple-element.26), kind=kOutput, calls=%fused_computation.4 | convolution fusion | flops 6455033856 | bytes 22548480 | tf_op jit(solution)/shard_map/dot_general | solution.py:82
  159.9 14.7 %add_convert_fusion = bf16[4096,768]{1,0:T(8,128)(2,1)} fusion(f32[4096,768]{1,0:T(8,128)S(1)} %fusion, bf16[1024,768]{1,0:T(8,128)(2,1)S(1)} %bitcast.77, bf16[1024,4096]{1,0:T(8,128)(2,1)} %collective-permute-done.6, f32[1024]{0:T(1024)S(1)} %get-tuple-element.24), kind=kOutput, calls=%fused_computation.3 | convolution fusion | flops 6461325312 | bytes 28839936 | tf_op jit(solution)/shard_map/dot_general | solution.py:82
  174.6 1.6 copy.36
  177.0 11.1 %multiply_reduce_fusion.1 = f32[1024]{0:T(1024)S(1)} fusion(bf16[1024,768]{0,1:T(8,128)(2,1)S(1)} %copy.35, bf16[1024,4096]{1,0:T(8,128)(2,1)} %all-gather.2.cloned.1.call-done, bf16[4096,768]{1,0:T(8,128)(2,1)} %bitcast.75), kind=kOutput, calls=%fused_computation.9 | convolution fusion | flops 6444809216 | bytes 16257024 | tf_op jit(solution)/shard_map/dot_general | solution.py:87
  188.2 11.5 %multiply_reduce_fusion = f32[1024]{0:T(1024)S(1)} fusion(bf16[1024,768]{0,1:T(8,128)(2,1)S(1)} %copy-done.4, bf16[1024,4096]{1,0:T(8,128)(2,1)} %collective-permute-done.6, bf16[4096,768]{1,0:T(8,128)(2,1)} %bitcast.76), kind=kOutput, calls=%fused_computation.8 | convolution fusion | flops 6444809216 | bytes 16257024 | tf_op jit(solution)/shard_map/dot_general | solution.py:87
  199.7 11.4 %all_to_all.22 = f32[16,1,128]{2,1,0:T(1,128)S(1)} all-to-all(f32[16,1,128]{2,1,0:T(1,128)S(1)} %bitcast.86), channel_id=1, replica_groups=mesh['x'=4,'y'=4,'z'=8,'core'=2] {'z','core'}, dimensions={0} | all-to-all | bytes 16384 | tf_op jit(solution)/shard_map/all_to_all | solution.py:101
  211.7 46.6 %reduce-scatter.2.cloned.1.call-done = bf16[256,768]{1,0:T(8,128)(2,1)} async-done(((bf16[4096,768]{1,0:T(8,128)(2,1)}), bf16[256,768]{1,0:T(8,128)(2,1)}) %reduce-scatter.2.cloned.1.call-update) | async-done | bytes 393232 | tf_op jit(solution)/shard_map/reduce_scatter | solution.py:93
  258.3 1.9 bitcast_convert_fusion
  (68 shorter events, 15.6 us)
Async XLA Ops:
  7.2 30.9 %copy-start = (bf16[128,8,768]{2,1,0:T(8,128)(2,1)S(1)}, bf16[128,8,768]{2,1,0:T(8,128)(2,1)}, u32[]{:S(2)}) copy-start(bf16[128,8,768]{2,1,0:T(8,128)(2,1)} %param.5) | copy-start | bytes 4718596
  7.2 25.7 %copy-start.5 = (bf16[1,256,768]{2,1,0:T(8,128)(2,1)S(1)}, bf16[1,256,768]{2,1,0:T(8,128)(2,1)}, u32[]{:S(2)}) copy-start(bf16[1,256,768]{2,1,0:T(8,128)(2,1)} %param.9) | copy-start | bytes 1179652
  7.2 138.9 %all-gather.2.cloned.1.call-start = ((), (), s32[]{:S(2)}) async-start(), calls=%async_computation.4 | async-start | bytes 9437184 | tf_op jit(solution)/shard_map/all_gather | solution.py:42
  7.9 20.1 %collective-permute-start = (bf16[256,768]{1,0:T(8,128)(2,1)}, bf16[256,768]{1,0:T(8,128)(2,1)S(1)}, u32[]{:S(2)}, u32[]{:S(2)}) collective-permute-start(bf16[256,768]{1,0:T(8,128)(2,1)} %bitcast.81), channel_id=1, source_target_pairs={{0,48},{16,0},{32,16},{48,32},{1,49},{17,1},{33,17},{49,33},{2,50}... | collective-permute-start | bytes 1179656 | tf_op jit(solution)/shard_map/ppermute | solution.py:49
  11.6 16.5 %collective-permute-start.1 = (bf16[256,768]{1,0:T(8,128)(2,1)}, bf16[256,768]{1,0:T(8,128)(2,1)S(1)}, u32[]{:S(2)}, u32[]{:S(2)}) collective-permute-start(bf16[256,768]{1,0:T(8,128)(2,1)} %bitcast.82), channel_id=1, source_target_pairs={{0,32},{16,48},{32,0},{48,16},{1,33},{17,49},{33,1},{49,17},{2,34}... | collective-permute-start | bytes 1179656 | tf_op jit(solution)/shard_map/ppermute | solution.py:49
  11.9 20.9 %collective-permute-start.2 = (bf16[256,768]{1,0:T(8,128)(2,1)}, bf16[256,768]{1,0:T(8,128)(2,1)S(1)}, u32[]{:S(2)}, u32[]{:S(2)}) collective-permute-start(bf16[256,768]{1,0:T(8,128)(2,1)} %bitcast.83), channel_id=1, source_target_pairs={{0,16},{16,32},{32,48},{48,0},{1,17},{17,33},{33,49},{49,1},{2,18}... | collective-permute-start | bytes 1179656 | tf_op jit(solution)/shard_map/ppermute | solution.py:49
  15.8 28.9 %all-to-all-start.1 = ((f32[16,2,128]{2,1,0:T(2,128)}), f32[16,2,128]{2,1,0:T(2,128)S(1)}, u32[]{:S(2)}, u32[]{:S(2)}) async-start(f32[16,2,128]{2,1,0:T(2,128)} %copy.33), calls=%async_computation.1 | async-start | bytes 32768 | tf_op jit(solution)/shard_map/all_to_all | solution.py:44
  34.9 69.7 %collective-permute-start.3 = (bf16[4,256,768]{2,1,0:T(8,128)(2,1)}, bf16[4,256,768]{2,1,0:T(8,128)(2,1)}, u32[]{:S(2)}, u32[]{:S(2)}) collective-permute-start(bf16[4,256,768]{2,1,0:T(8,128)(2,1)} %get-tuple-element.18), channel_id=1, source_target_pairs={{0,192},{64,0},{128,64},{192,128},{1,193},{65,1},{129,65},{193,129... | collective-permute-start | bytes 4718600 | tf_op jit(solution)/shard_map/ppermute | solution.py:49
  37.4 69.9 %collective-permute-start.4 = (bf16[4,256,768]{2,1,0:T(8,128)(2,1)}, bf16[4,256,768]{2,1,0:T(8,128)(2,1)}, u32[]{:S(2)}, u32[]{:S(2)}) collective-permute-start(bf16[4,256,768]{2,1,0:T(8,128)(2,1)} %get-tuple-element.18), channel_id=1, source_target_pairs={{0,128},{64,192},{128,0},{192,64},{1,129},{65,193},{129,1},{193,65... | collective-permute-start | bytes 4718600 | tf_op jit(solution)/shard_map/ppermute | solution.py:49
  42.6 67.4 %collective-permute-start.5 = (bf16[4,256,768]{2,1,0:T(8,128)(2,1)}, bf16[4,256,768]{2,1,0:T(8,128)(2,1)S(1)}, u32[]{:S(2)}, u32[]{:S(2)}) collective-permute-start(bf16[4,256,768]{2,1,0:T(8,128)(2,1)} %get-tuple-element.18), channel_id=1, source_target_pairs={{0,64},{64,128},{128,192},{192,0},{1,65},{65,129},{129,193},{193,1... | collective-permute-start | bytes 4718600 | tf_op jit(solution)/shard_map/ppermute | solution.py:49
  44.7 81.9 %all-to-all-start = ((bf16[16,72,768]{2,1,0:T(8,128)(2,1)}), bf16[16,72,768]{2,1,0:T(8,128)(2,1)S(1)}, u32[]{:S(2)}, u32[]{:S(2)}) async-start(bf16[16,72,768]{2,1,0:T(8,128)(2,1)} %broadcast_select_fusion), calls=%async_computation | async-start | bytes 3538944 | tf_op jit(solution)/shard_map/all_to_all | solution.py:43
  54.5 203.9 %reduce-scatter.2.cloned.1.call-start = ((), (), s32[]{:S(2)}) async-start(), calls=%async_computation.5 | async-start | bytes 6684672 | tf_op jit(solution)/shard_map/reduce_scatter | solution.py:93
  146.1 13.8 %collective-permute-start.6 = (bf16[1024,4096]{1,0:T(8,128)(2,1)}, bf16[1024,4096]{1,0:T(8,128)(2,1)}, u32[]{:S(2)}, u32[]{:S(2)}) collective-permute-start(bf16[1024,4096]{1,0:T(8,128)(2,1)} %all-gather.2.cloned.1.call-done), channel_id=1, source_target_pairs={{0,1},{1,0},{2,3},{3,2},{4,5},{5,4},{6,7},{7,6},{8,9},{9,8},{10,11... | collective-permute-start | bytes 25165832 | tf_op jit(solution)/shard_map/ppermute | solution.py:56
  148.0 10.8 %copy-start.2 = (bf16[8,128,768]{2,1,0:T(8,128)(2,1)}, bf16[8,128,768]{2,1,0:T(8,128)(2,1)S(1)}, u32[]{:S(2)}) copy-start(bf16[8,128,768]{2,1,0:T(8,128)(2,1)S(1)} %convolution_convert_fusion.1) | copy-start | bytes 4718596
  174.6 1.7 copy-start.3
  177.0 11.1 %copy-start.4 = (bf16[1024,768]{0,1:T(8,128)(2,1)S(1)}, bf16[1024,768]{0,1:T(8,128)(2,1)}, u32[]{:S(2)}) copy-start(bf16[1024,768]{0,1:T(8,128)(2,1)} %copy.36) | copy-start | bytes 4718596
  188.1 23.0 %copy-start.6 = (s32[128,8]{0,1:T(8,128)S(1)}, s32[128,8]{0,1:T(8,128)}, u32[]{:S(2)}) copy-start(s32[128,8]{0,1:T(8,128)} %param.8) | copy-start | bytes 12292
  188.1 72.1 %copy-start.1 = (bf16[128,8,768]{2,1,0:T(8,128)(2,1)S(1)}, bf16[128,8,768]{2,1,0:T(8,128)(2,1)}, u32[]{:S(2)}) copy-start(bf16[128,8,768]{2,1,0:T(8,128)(2,1)} %param.5) | copy-start | bytes 4718596
Sparse Core Ops, SparseCore 0:
  9.8 136.2 all-gather.1
  174.7 83.5 reduce-scatter.1
where the time goes:
time: 268 us; the launch traced here: 267 us
  waiting for transfers between devices  123 us (46%)
  matrix products  49.3 us (18%)
  local copies, waits for them, and re-layouts  33.2 us (12%)
  starting transfers between devices  28.9 us (11%)
  between operations  14.4 us (5%)
  blocking collectives  11.4 us (4%)
  other arithmetic  7.23 us (3%)
    ppermute x6, waiting for transfers between devices, ring_gather(): lax.ppermute(x, axis, perm=[(i, (i - d) % n) for i in range(n)])  54.9 us
    reduce_scatter x1, waiting for transfers between devices, body(): lax.psum_scatter(partial, ('x', 'y'), scatter_dimension=0, tiled=True)  46.6 us
    dot_general x2, matrix products, part(): lax.dot_general(scaled, h_c, (((0,), (0,)), ((), ())), preferred_element_...  25.4 us
    dot_general x2, matrix products, score(): lax.dot_general(dy_c, w_full, (((1,), (0,)), ((), ())), preferred_element...  22.6 us
    all_gather x1, waiting for transfers between devices, body(): dy_z = lax.all_gather(upstream, 'z', axis=0, tiled=True)  19.4 us
    unnamed x28, local copies, waits for them, and re-layouts  17.8 us
    all_to_all x1, blocking collectives, body(): lax.all_to_all(by_source, ez, split_axis=0, concat_axis=0, tiled=True)  11.4 us
    all_to_all x1, starting transfers between devices, body(): lax.all_to_all(send_meta, ez, split_axis=0, concat_axis=0, tiled=True)  9.99 us
  transfers between devices with their start and end apart: 11, of which 5 were waited for; matrix products, arithmetic and copies ran while one was open for 27% of the time, Pallas kernels for 0%

commit v1 on v0

--- a/solution.py
+++ b/solution.py
@@ -2,6 +2,7 @@
 import jax.numpy as jnp
 from jax import lax
 from jax.sharding import Mesh, PartitionSpec as P
+from jax.lax import all_to_all, axis_size
 
 
 def body(hidden, upstream, probs, expert_ids, w_down):
@@ -39,7 +40,10 @@
     )
     inv = jnp.where(routed, slot_place, -1).astype(jnp.float32)
     send_meta = jnp.stack([p_tok.T, inv.T], axis=1)
-    dy_z = lax.all_gather(upstream, "z", axis=0, tiled=True)
+    all_rows = all_to_all(
+        jnp.stack([upstream] * axis_size("z"), 0), axis_name="z", split_axis=0, concat_axis=0
+    )
+    dy_z = jnp.concatenate(all_rows, 0)
     recv_h = lax.all_to_all(send_h, ez, split_axis=0, concat_axis=0, tiled=True)
     recv_meta = lax.all_to_all(send_meta, ez, split_axis=0, concat_axis=0, tiled=True)
 

time: 268 us -> 395 us (1.47)
  waiting for transfers between devices: 123 us -> 202 us
  blocking collectives: 11.4 us -> 61 us
  starting transfers between devices: 28.9 us -> 23.1 us
  local copies, waits for them, and re-layouts: 33.2 us -> 37.4 us
    all_to_all x1, waiting for transfers between devices: 0.01 us -> 69.4 us  [body(): all_to_all(jnp.stack([upstream] * axis_size('z'), 0), axis_name='z', spli...]
    all_to_all x0 -> x1, blocking collectives: none -> 51.2 us  [body(): recv_h = lax.all_to_all(send_h, ez, split_axis=0, concat_axis=0, tiled=True)]
    ppermute x6, waiting for transfers between devices: 54.9 us -> 85.8 us  [ring_gather(): lax.ppermute(x, axis, perm=[(i, (i - d) % n) for i in range(n)])]
    all_gather x1 -> x0, waiting for transfers between devices: 19.4 us -> none  [body(): dy_z = lax.all_gather(upstream, 'z', axis=0, tiled=True)]
    all_to_all x1, starting transfers between devices: 9.71 us -> 5.15 us  [body(): all_to_all(jnp.stack([upstream] * axis_size('z'), 0), axis_name='z', spli...]
    another operation x0 -> x1, local copies, waits for them, and re-layouts: none -> 4.41 us  [body(): jnp.stack([upstream] * axis_size('z'), 0)]
    unnamed x28 -> x30, local copies, waits for them, and re-layouts: 17.8 us -> 16.3 us
  transfers between devices with their start and end apart: 11 -> 10, of which waited for: 5 -> 7; matrix products, arithmetic and copies ran while one was open for 27% -> 18% of each run, Pallas kernels for 0% -> 0%
where the time goes in v1:
time: 395 us
  waiting for transfers between devices  202 us (51%)
  blocking collectives  61 us (15%)
  matrix products  49.2 us (12%)
  local copies, waits for them, and re-layouts  37.4 us (9%)
  starting transfers between devices  23.1 us (6%)
  between operations  14.3 us (4%)
  other arithmetic  7.36 us (2%)
    ppermute x6, waiting for transfers between devices, ring_gather(): lax.ppermute(x, axis, perm=[(i, (i - d) % n) for i in range(n)])  85.8 us
    all_to_all x1, waiting for transfers between devices, body(): all_to_all(jnp.stack([upstream] * axis_size('z'), 0), axis_name='z', spli...  69.4 us
    all_to_all x1, blocking collectives, body(): recv_h = lax.all_to_all(send_h, ez, split_axis=0, concat_axis=0, tiled=True)  51.2 us
    reduce_scatter x1, waiting for transfers between devices, body(): lax.psum_scatter(partial, ('x', 'y'), scatter_dimension=0, tiled=True)  46 us
    dot_general x2, matrix products, part(): lax.dot_general(scaled, h_c, (((0,), (0,)), ((), ())), preferred_element_...  25.3 us
    dot_general x2, matrix products, score(): lax.dot_general(dy_c, w_full, (((1,), (0,)), ((), ())), preferred_element...  22.6 us
    unnamed x30, local copies, waits for them, and re-layouts  16.3 us
    all_to_all x1, starting transfers between devices, body(): lax.all_to_all(send_meta, ez, split_axis=0, concat_axis=0, tiled=True)  9.98 us
  transfers between devices with their start and end apart: 10, of which 7 were waited for; matrix products, arithmetic and copies ran while one was open for 18% of the time, Pallas kernels for 0%

profile of v1, /device:TPU:1, one launch (start us, length us, event | category | flops | bytes accessed | tf_op | source)
XLA Modules:
  0.0 394.8 jit_solution(5444107076643737104)
XLA Ops:
  10.5 10.0 %all-to-all-start.2 = ((f32[16,2,128]{2,1,0:T(2,128)}), f32[16,2,128]{2,1,0:T(2,128)S(1)}, u32[]{:S(2)}, u32[]{:S(2)}) async-start(f32[16,2,128]{2,1,0:T(2,128)} %copy.33), calls=%async_computation.2 | async-start | bytes 32768 | tf_op jit(solution)/shard_map/all_to_all | solution.py:48
  21.7 4.6 %gather_fusion = bf16[1152,768]{1,0:T(8,128)(2,1)S(1)} fusion(bf16[1024,768]{1,0:T(8,128)(2,1)S(1)} %bitcast.72, s32[2048]{0:T(1024)S(1)} %pad_clamp_fusion), kind=kCustom, calls=%fused_computation | custom fusion | bytes 3543552 | tf_op jit(solution)/shard_map/gather | solution.py:33
  27.8 51.2 %all_to_all.27 = bf16[16,72,768]{2,1,0:T(8,128)(2,1)S(1)} all-to-all(bf16[16,72,768]{2,1,0:T(8,128)(2,1)} %broadcast_select_fusion), channel_id=1, replica_groups=mesh['x'=4,'y'=4,'z'=8,'core'=2] {'z','core'}, dimensions={0} | all-to-all | bytes 3538944 | tf_op jit(solution)/shard_map/all_to_all | solution.py:47
  79.1 4.4 %stack.48 = bf16[8,128,4096]{2,1,0:T(8,128)(2,1)} broadcast(bf16[128,4096]{1,0:T(8,128)(2,1)S(1)} %copy-done.6), dimensions={1,2} | broadcast | bytes 9437184 | tf_op jit(solution)/shard_map/stack | solution.py:44
  83.5 5.2 %all-to-all-start = ((bf16[8,128,4096]{2,1,0:T(8,128)(2,1)}), bf16[8,128,4096]{2,1,0:T(8,128)(2,1)}, u32[]{:S(2)}, u32[]{:S(2)}) async-start(bf16[8,128,4096]{2,1,0:T(8,128)(2,1)} %stack.48), calls=%async_computation | async-start | bytes 16777216 | tf_op jit(solution)/shard_map/all_to_all | solution.py:43
  88.7 2.8 collective-permute-start
  92.6 16.1 %collective-permute-done = bf16[256,768]{1,0:T(8,128)(2,1)S(1)} collective-permute-done((bf16[256,768]{1,0:T(8,128)(2,1)S(1)}, bf16[256,768]{1,0:T(8,128)(2,1)S(1)}, u32[]{:S(2)}, u32[]{:S(2)}) %collective-permute-start) | collective-permute-done | bytes 393248 | tf_op jit(solution)/shard_map/ppermute | solution.py:53
  108.7 3.9 collective-permute-done.2
  114.2 2.5 collective-permute-start.3
  117.8 65.9 %collective-permute-done.3 = bf16[4,256,768]{2,1,0:T(8,128)(2,1)} collective-permute-done((bf16[4,256,768]{2,1,0:T(8,128)(2,1)S(1)}, bf16[4,256,768]{2,1,0:T(8,128)(2,1)}, u32[]{:S(2)}, u32[]{:S(2)}) %collective-permute-start.3) | collective-permute-done | bytes 1572896 | tf_op jit(solution)/shard_map/ppermute | solution.py:53
  183.6 2.7 bitcast_dynamic-update-slice_fusion.4
  186.3 2.6 bitcast_dynamic-update-slice_fusion.2
  188.9 2.7 bitcast_dynamic-update-slice_fusion
  192.9 2.7 bitcast_dynamic-update-slice_fusion.5
  195.6 2.7 bitcast_dynamic-update-slice_fusion.3
  198.3 2.6 bitcast_dynamic-update-slice_fusion.1
  200.9 6.0 %constant_dynamic-slice_fusion.2 = bf16[4,4,256,768]{3,2,1,0:T(8,128)(2,1)} fusion(bf16[8,4,256,768]{3,2,1,0:T(8,128)(2,1)} %bitcast_dynamic-update-slice_fusion.1, s32[]{:T(128)S(6)} %select_n.102), kind=kLoop, calls=%fused_computation.71 | loop fusion | bytes 12582916 | tf_op jit(solution)/shard_map/jit(_roll_dynamic)/dynamic_slice | solution.py:55
  206.9 69.4 %all-to-all-done = bf16[8,128,4096]{2,1,0:T(8,128)(2,1)} async-done(((bf16[8,128,4096]{2,1,0:T(8,128)(2,1)}), bf16[8,128,4096]{2,1,0:T(8,128)(2,1)}, u32[]{:S(2)}, u32[]{:S(2)}) %all-to-all-start) | async-done | bytes 8388640 | tf_op jit(solution)/shard_map/all_to_all | solution.py:43
  278.1 10.8 %fusion = f32[4096,768]{1,0:T(8,128)S(1)} fusion(bf16[1024,768]{1,0:T(8,128)(2,1)S(1)} %bitcast.80, bf16[1024,4096]{1,0:T(8,128)(2,1)} %bitcast, f32[1024]{0:T(1024)S(1)} %get-tuple-element.26), kind=kOutput, calls=%fused_computation.4 | convolution fusion | flops 6455033856 | bytes 22548480 | tf_op jit(solution)/shard_map/dot_general | solution.py:86
  289.9 14.6 %add_convert_fusion = bf16[4096,768]{1,0:T(8,128)(2,1)} fusion(f32[4096,768]{1,0:T(8,128)S(1)} %fusion, bf16[1024,768]{1,0:T(8,128)(2,1)S(1)} %bitcast.78, bf16[1024,4096]{1,0:T(8,128)(2,1)} %collective-permute-done.6, f32[1024]{0:T(1024)S(1)} %get-tuple-element.24), kind=kOutput, calls=%fused_computation.3 | convolution fusion | flops 6461325312 | bytes 28839936 | tf_op jit(solution)/shard_map/dot_general | solution.py:86
  307.0 11.1 %multiply_reduce_fusion.1 = f32[1024]{0:T(1024)S(1)} fusion(bf16[1024,768]{0,1:T(8,128)(2,1)S(1)} %copy.35, bf16[1024,4096]{1,0:T(8,128)(2,1)} %bitcast, bf16[4096,768]{1,0:T(8,128)(2,1)} %bitcast.76), kind=kOutput, calls=%fused_computation.9 | convolution fusion | flops 6444809216 | bytes 16257024 | tf_op jit(solution)/shard_map/dot_general | solution.py:91
  318.1 11.5 %multiply_reduce_fusion = f32[1024]{0:T(1024)S(1)} fusion(bf16[1024,768]{0,1:T(8,128)(2,1)S(1)} %copy-done.4, bf16[1024,4096]{1,0:T(8,128)(2,1)} %collective-permute-done.6, bf16[4096,768]{1,0:T(8,128)(2,1)} %bitcast.77), kind=kOutput, calls=%fused_computation.8 | convolution fusion | flops 6444809216 | bytes 16257024 | tf_op jit(solution)/shard_map/dot_general | solution.py:91
  329.6 9.8 %all_to_all.28 = f32[16,1,128]{2,1,0:T(1,128)S(1)} all-to-all(f32[16,1,128]{2,1,0:T(1,128)S(1)} %bitcast.87), channel_id=1, replica_groups=mesh['x'=4,'y'=4,'z'=8,'core'=2] {'z','core'}, dimensions={0} | all-to-all | bytes 16384 | tf_op jit(solution)/shard_map/all_to_all | solution.py:105
  340.0 46.0 %reduce-scatter.2.cloned.1.call-done = bf16[256,768]{1,0:T(8,128)(2,1)} async-done(((bf16[4096,768]{1,0:T(8,128)(2,1)}), bf16[256,768]{1,0:T(8,128)(2,1)}) %reduce-scatter.2.cloned.1.call-update) | async-done | bytes 393232 | tf_op jit(solution)/shard_map/reduce_scatter | solution.py:97
  (69 shorter events, 18.9 us)
Async XLA Ops:
  7.2 14.5 %copy-start = (bf16[128,8,768]{2,1,0:T(8,128)(2,1)S(1)}, bf16[128,8,768]{2,1,0:T(8,128)(2,1)}, u32[]{:S(2)}) copy-start(bf16[128,8,768]{2,1,0:T(8,128)(2,1)} %param.5) | copy-start | bytes 4718596
  10.5 17.3 %all-to-all-start.2 = ((f32[16,2,128]{2,1,0:T(2,128)}), f32[16,2,128]{2,1,0:T(2,128)S(1)}, u32[]{:S(2)}, u32[]{:S(2)}) async-start(f32[16,2,128]{2,1,0:T(2,128)} %copy.33), calls=%async_computation.2 | async-start | bytes 32768 | tf_op jit(solution)/shard_map/all_to_all | solution.py:48
  27.7 51.4 %copy-start.6 = (bf16[128,4096]{1,0:T(8,128)(2,1)S(1)}, bf16[128,4096]{1,0:T(8,128)(2,1)}, u32[]{:S(2)}) copy-start(bf16[128,4096]{1,0:T(8,128)(2,1)} %param.6) | copy-start | bytes 3145732
  83.5 5.2 %copy-start.5 = (bf16[1,256,768]{2,1,0:T(8,128)(2,1)S(1)}, bf16[1,256,768]{2,1,0:T(8,128)(2,1)}, u32[]{:S(2)}) copy-start(bf16[1,256,768]{2,1,0:T(8,128)(2,1)} %param.9) | copy-start | bytes 1179652
  83.5 192.8 %all-to-all-start = ((bf16[8,128,4096]{2,1,0:T(8,128)(2,1)}), bf16[8,128,4096]{2,1,0:T(8,128)(2,1)}, u32[]{:S(2)}, u32[]{:S(2)}) async-start(bf16[8,128,4096]{2,1,0:T(8,128)(2,1)} %stack.48), calls=%async_computation | async-start | bytes 16777216 | tf_op jit(solution)/shard_map/all_to_all | solution.py:43
  88.6 297.4 %reduce-scatter.2.cloned.1.call-start = ((), (), s32[]{:S(2)}) async-start(), calls=%async_computation.5 | async-start | bytes 6684672 | tf_op jit(solution)/shard_map/reduce_scatter | solution.py:97
  88.7 20.0 %collective-permute-start = (bf16[256,768]{1,0:T(8,128)(2,1)S(1)}, bf16[256,768]{1,0:T(8,128)(2,1)S(1)}, u32[]{:S(2)}, u32[]{:S(2)}) collective-permute-start(bf16[256,768]{1,0:T(8,128)(2,1)S(1)} %bitcast.82), channel_id=1, source_target_pairs={{0,48},{16,0},{32,16},{48,32},{1,49},{17,1},{33,17},{49,33},{2,50}... | collective-permute-start | bytes 1179656 | tf_op jit(solution)/shard_map/ppermute | solution.py:53
  91.5 17.2 %collective-permute-start.1 = (bf16[256,768]{1,0:T(8,128)(2,1)S(1)}, bf16[256,768]{1,0:T(8,128)(2,1)S(1)}, u32[]{:S(2)}, u32[]{:S(2)}) collective-permute-start(bf16[256,768]{1,0:T(8,128)(2,1)S(1)} %bitcast.83), channel_id=1, source_target_pairs={{0,32},{16,48},{32,0},{48,16},{1,33},{17,49},{33,1},{49,17},{2,34}... | collective-permute-start | bytes 1179656 | tf_op jit(solution)/shard_map/ppermute | solution.py:53
  91.9 20.8 %collective-permute-start.2 = (bf16[256,768]{1,0:T(8,128)(2,1)S(1)}, bf16[256,768]{1,0:T(8,128)(2,1)S(1)}, u32[]{:S(2)}, u32[]{:S(2)}) collective-permute-start(bf16[256,768]{1,0:T(8,128)(2,1)S(1)} %bitcast.84), channel_id=1, source_target_pairs={{0,16},{16,32},{32,48},{48,0},{1,17},{17,33},{33,49},{49,1},{2,18}... | collective-permute-start | bytes 1179656 | tf_op jit(solution)/shard_map/ppermute | solution.py:53
  114.2 69.5 %collective-permute-start.3 = (bf16[4,256,768]{2,1,0:T(8,128)(2,1)S(1)}, bf16[4,256,768]{2,1,0:T(8,128)(2,1)}, u32[]{:S(2)}, u32[]{:S(2)}) collective-permute-start(bf16[4,256,768]{2,1,0:T(8,128)(2,1)S(1)} %get-tuple-element.18), channel_id=1, source_target_pairs={{0,192},{64,0},{128,64},{192,128},{1,193},{65,1},{129,65},{193,129... | collective-permute-start | bytes 4718600 | tf_op jit(solution)/shard_map/ppermute | solution.py:53
  116.6 69.7 %collective-permute-start.4 = (bf16[4,256,768]{2,1,0:T(8,128)(2,1)S(1)}, bf16[4,256,768]{2,1,0:T(8,128)(2,1)}, u32[]{:S(2)}, u32[]{:S(2)}) collective-permute-start(bf16[4,256,768]{2,1,0:T(8,128)(2,1)S(1)} %get-tuple-element.18), channel_id=1, source_target_pairs={{0,128},{64,192},{128,0},{192,64},{1,129},{65,193},{129,1},{193,65... | collective-permute-start | bytes 4718600 | tf_op jit(solution)/shard_map/ppermute | solution.py:53
  117.2 71.8 %collective-permute-start.5 = (bf16[4,256,768]{2,1,0:T(8,128)(2,1)S(1)}, bf16[4,256,768]{2,1,0:T(8,128)(2,1)}, u32[]{:S(2)}, u32[]{:S(2)}) collective-permute-start(bf16[4,256,768]{2,1,0:T(8,128)(2,1)S(1)} %get-tuple-element.18), channel_id=1, source_target_pairs={{0,64},{64,128},{128,192},{192,0},{1,65},{65,129},{129,193},{193,1... | collective-permute-start | bytes 4718600 | tf_op jit(solution)/shard_map/ppermute | solution.py:53
  276.3 13.6 %collective-permute-start.6 = (bf16[1024,4096]{1,0:T(8,128)(2,1)}, bf16[1024,4096]{1,0:T(8,128)(2,1)}, u32[]{:S(2)}, u32[]{:S(2)}) collective-permute-start(bf16[1024,4096]{1,0:T(8,128)(2,1)} %bitcast), channel_id=1, source_target_pairs={{0,1},{1,0},{2,3},{3,2},{4,5},{5,4},{6,7},{7,6},{8,9},{9,8},{10,11... | collective-permute-start | bytes 25165832 | tf_op jit(solution)/shard_map/ppermute | solution.py:60
  278.0 10.8 %copy-start.2 = (bf16[8,128,768]{2,1,0:T(8,128)(2,1)}, bf16[8,128,768]{2,1,0:T(8,128)(2,1)S(1)}, u32[]{:S(2)}) copy-start(bf16[8,128,768]{2,1,0:T(8,128)(2,1)S(1)} %convolution_convert_fusion.1) | copy-start | bytes 4718596
  304.5 1.7 copy-start.3
  307.0 11.1 %copy-start.4 = (bf16[1024,768]{0,1:T(8,128)(2,1)S(1)}, bf16[1024,768]{0,1:T(8,128)(2,1)}, u32[]{:S(2)}) copy-start(bf16[1024,768]{0,1:T(8,128)(2,1)} %copy.36) | copy-start | bytes 4718596
  318.1 21.3 %copy-start.7 = (s32[128,8]{0,1:T(8,128)S(1)}, s32[128,8]{0,1:T(8,128)}, u32[]{:S(2)}) copy-start(s32[128,8]{0,1:T(8,128)} %param.8) | copy-start | bytes 12292
  318.1 69.8 %copy-start.1 = (bf16[128,8,768]{2,1,0:T(8,128)(2,1)S(1)}, bf16[128,8,768]{2,1,0:T(8,128)(2,1)}, u32[]{:S(2)}) copy-start(bf16[128,8,768]{2,1,0:T(8,128)(2,1)} %param.5) | copy-start | bytes 4718596
Sparse Core Ops, SparseCore 0:
  304.6 81.3 reduce-scatter.1
